TPU v7x, 512 devices: a whole 4x8x8 slice. The times are simulated.
512 devices in a mesh: grp: 16 (over z, core), dev: 32 (over x, y).
Axes of the slice: x: 4, y: 8, z: 8, core: 2. Of those that a mesh axis runs over, the one named last changes fastest.
Arguments:
- ssm_input: bfloat16 [4096, 4096], P('grp', 'dev'), may hold values from -6 to 6
- gate_input: bfloat16 [4096, 4096], P('grp', 'dev'), may hold values from -6 to 6
- step_size: float32 [4096, 64], P('grp', 'dev'), may hold values from 6.1035156e-05 to 0.3375
- decay_rate: float32 [64], P('dev'), may hold values from 0.5 to 2
- in_coeff: bfloat16 [4096, 128], P('grp'), may hold values from -6 to 6
- out_coeff: bfloat16 [4096, 128], P('grp'), may hold values from -6 to 6
- skip_gain: float32 [64], P('dev'), may hold values from 0.5 to 3
- norm_gain: float32 [4096], P('dev'), may hold values from 0.5 to 1.5
- out_proj: bfloat16 [4096, 2048], P(None, 'dev'), may hold values from -0.09375 to 0.09375
- residual: bfloat16 [4096, 2048], P(('grp', 'dev')), may hold values from -6 to 6
- ffn_gain: float32 [2048], replicated, may hold values from 0.5 to 1.5
- router: float32 [2048, 16], replicated, may hold values from -0.125 to 0.125
- routes: int32 [4096, 2], P(('grp', 'dev')), may hold values from 0 to 15, all different within a row; in each aligned block of 8 rows (0 to 7, 8 to 15, ...) at most 2 rows name the same one
- gate_weight: bfloat16 [16, 2048, 8192], P('grp', None, 'dev'), may hold values from -0.125 to 0.125
- up_weight: bfloat16 [16, 2048, 8192], P('grp', None, 'dev'), may hold values from -0.125 to 0.125
- down_weight: bfloat16 [16, 8192, 2048], P('grp', 'dev'), may hold values from -0.0625 to 0.0625
Outputs:
- moe_out: bfloat16 [4096, 2048], P(('grp', 'dev'))
Inputs may be any that keep to these rules, and one draw needn't show every extreme that they name: `routes`: each row names two different experts; among the 8 rows of one dispatch block of consecutive tokens no expert is named more than 2 times, a bound that some block reaches.
All inputs are finite; a program needn't handle non-finite values.
Results may differ from a plain program's by a relative error of at most 0.012.
Values may be sent and summed in bfloat16 or wider, within the bound.
No kernel may reach another device: no remote copies, remote signals or barrier semaphores. Data moves between devices by JAX's collectives and lax.ppermute only.
A program may use at most 64 MiB of HBM per device.

v0:
```python
import jax
import jax.numpy as jnp
from jax import lax
from jax.sharding import Mesh
from jax.sharding import PartitionSpec as P

DEV = ("dev_0", "dev_1")
GRP_DEV = ("grp", "dev_0", "dev_1")
EPSILON = 1e-05
HIGHEST_PREC = lax.Precision.HIGHEST


def side_by_side(arrays, axis, dim, along):
    columns = [a.reshape(*a.shape[:along], -1) for a in arrays]
    both = jnp.concatenate(columns, axis=along)
    filled, at, finished = (lax.all_gather(both, axis, axis=dim, tiled=True), 0, [])
    for a, column in zip(arrays, columns):
        piece = filled[..., at : at + column.shape[along]]
        finished.append(piece.reshape(*piece.shape[:along], *a.shape[along:]))
        at += column.shape[along]
    return tuple(finished)


def sent_to_all(shard, axis):
    peers = lax.axis_size(axis)
    return lax.all_to_all(
        jnp.broadcast_to(shard[None], (peers, *shard.shape)), axis, 0, 0, tiled=True
    )


def of_everyone(shard, axis):
    everything = sent_to_all(shard, axis)
    return jnp.sum(everything, axis=0)


def in_order(tiles, dim):
    dims = list(tiles.shape[1:])
    dims[dim] *= tiles.shape[0]
    return jnp.moveaxis(tiles, 0, dim).reshape(dims)


def collect(shard, axis, dim):
    return in_order(sent_to_all(shard, axis), dim)


def sum_by_axis(terms, axes):
    total = terms.astype(jnp.bfloat16)
    total = lax.psum_scatter(total, axes, scatter_dimension=0, tiled=True)
    return total.astype(jnp.float32)


def rms_scale(values, gain_vec):
    return (
        values * lax.rsqrt(jnp.mean(values * values, axis=-1, keepdims=True) + EPSILON) * gain_vec
    )


def slot_tables(routes_block, expert_count, slot_cap):
    blocks, row_total = (routes_block.shape[0], routes_block.shape[1])
    flat_routes = routes_block.reshape(blocks, row_total * 2)
    onehot = (
        flat_routes[:, :, None] == jnp.arange(expert_count, dtype=jnp.int32)[None, None, :]
    ).astype(jnp.int32)
    earlier = jnp.cumsum(onehot, axis=1) - onehot
    slot_rank = jnp.sum(earlier * onehot, axis=2)
    slot_index = (flat_routes * slot_cap + slot_rank).reshape(blocks, row_total, 2)
    placed = (
        slot_index[:, :, :, None]
        == jnp.arange(expert_count * slot_cap, dtype=jnp.int32)[None, None, None, :]
    )
    return placed.astype(jnp.float32)


def shards(
    ssm_input,
    gate_input,
    step_size,
    decay_rate,
    in_coeff,
    out_coeff,
    skip_gain,
    norm_gain,
    out_proj,
    residual,
    ffn_gain,
    router,
    routes,
    gate_weight,
    up_weight,
    down_weight,
):
    tok_rows = ssm_input.shape[0]
    head_count = step_size.shape[1]
    head_width = ssm_input.shape[1] // head_count
    dev_count = lax.axis_size(DEV)
    inner_dim = ssm_input.shape[1] * dev_count
    block_rows = residual.shape[0]
    model_dim = residual.shape[1]
    experts = lax.axis_size("grp")
    slot_cap = max(2, 4 * block_rows // experts)
    group_slots = experts * slot_cap
    inputs_f = ssm_input.astype(jnp.float32).reshape(tok_rows, head_count, head_width)
    in_float = in_coeff.astype(jnp.float32)
    out_float = out_coeff.astype(jnp.float32)
    log_rate = -(step_size * decay_rate[None, :])
    cumulative = jnp.cumsum(log_rate, axis=0)
    causal = (jnp.arange(tok_rows)[:, None] >= jnp.arange(tok_rows)[None, :])[:, :, None]
    spread = cumulative[:, None, :] - cumulative[None, :, :]
    decay_pair = jnp.where(causal, jnp.exp(jnp.where(causal, spread, 0.0)), 0.0)
    scores = jnp.dot(out_coeff, in_coeff.T, preferred_element_type=jnp.float32)
    mixing = decay_pair * scores[:, :, None] * step_size[None, :, :]
    inside = jnp.einsum("tuh,uhp->thp", mixing, inputs_f, precision=HIGHEST_PREC)
    to_end = jnp.exp(cumulative[-1][None, :] - cumulative) * step_size
    own_state = jnp.einsum("uh,uhp,un->hpn", to_end, inputs_f, in_float, precision=HIGHEST_PREC)
    own_log = cumulative[-1]
    group_logs, group_states = tuple(
        (
            part.astype(jnp.float32)
            for part in side_by_side(
                (own_log[None].astype(jnp.bfloat16), own_state[None].astype(jnp.bfloat16)),
                "grp",
                0,
                2,
            )
        )
    )
    group_index = jnp.arange(group_logs.shape[0])
    my_group = lax.axis_index("grp")
    inclusive = jnp.cumsum(group_logs, axis=0)
    exclusive = inclusive - group_logs
    before_me = jnp.sum(jnp.where((group_index == my_group)[:, None], exclusive, 0.0), axis=0)
    earlier_mask = (group_index < my_group)[:, None]
    weighting = jnp.where(
        earlier_mask, jnp.exp(jnp.where(earlier_mask, before_me[None, :] - inclusive, 0.0)), 0.0
    )
    entering = jnp.einsum("gh,ghpn->hpn", weighting, group_states, precision=HIGHEST_PREC)
    carried = jnp.exp(cumulative)[:, :, None] * jnp.einsum(
        "hpn,tn->thp", entering, out_float, precision=HIGHEST_PREC
    )
    ssm_out = inside + carried + skip_gain[None, :, None] * inputs_f
    gated_out = ssm_out.reshape(tok_rows, head_count * head_width) * jax.nn.silu(
        gate_input.astype(jnp.float32)
    )
    squares = lax.psum(jnp.sum(gated_out * gated_out, axis=1), DEV)
    mixed_rows = (
        gated_out * lax.rsqrt(squares[:, None] / inner_dim + EPSILON) * norm_gain[None, :]
    ).astype(jnp.bfloat16)
    gathered = lax.all_gather(mixed_rows, DEV, axis=0)
    projected = jnp.einsum(
        "dtc,dcf->tf",
        gathered,
        out_proj.reshape(dev_count, -1, out_proj.shape[1]),
        preferred_element_type=jnp.float32,
    ).astype(jnp.bfloat16)
    mamba_out = lax.all_to_all(projected, DEV, split_axis=0, concat_axis=1, tiled=True)
    hidden_res = (residual.astype(jnp.float32) + mamba_out.astype(jnp.float32)).astype(jnp.bfloat16)
    hidden_float = hidden_res.astype(jnp.float32)
    normed = rms_scale(hidden_float, ffn_gain).astype(jnp.bfloat16)
    logits = jnp.dot(normed.astype(jnp.float32), router, precision=HIGHEST_PREC)
    expert_ids = jnp.arange(experts, dtype=jnp.int32)[None, :]
    first_logit = jnp.sum(logits * (routes[:, 0:1] == expert_ids).astype(jnp.float32), axis=1)
    second_logit = jnp.sum(logits * (routes[:, 1:2] == expert_ids).astype(jnp.float32), axis=1)
    first_prob = jax.nn.sigmoid(first_logit - second_logit)
    second_prob = 1.0 - first_prob
    placed = slot_tables(routes[None], experts, slot_cap)[0]
    filled = jnp.sum(placed, axis=1)
    outgoing = jnp.dot(
        filled.T.astype(jnp.bfloat16), normed, preferred_element_type=jnp.float32
    ).astype(jnp.bfloat16)
    outgoing = outgoing.reshape(experts, slot_cap, model_dim)
    arrived = lax.all_to_all(outgoing, "grp", split_axis=0, concat_axis=0, tiled=True)
    all_rows = lax.all_gather(arrived, DEV, axis=0, tiled=True).reshape(-1, model_dim)
    gate_act = jnp.dot(all_rows, gate_weight[0], preferred_element_type=jnp.float32)
    up_act = jnp.dot(all_rows, up_weight[0], preferred_element_type=jnp.float32)
    hidden = (jax.nn.silu(gate_act) * up_act).astype(jnp.bfloat16)
    summed = sum_by_axis(jnp.dot(hidden, down_weight[0], preferred_element_type=jnp.float32), DEV)
    returned = lax.all_to_all(
        summed.astype(jnp.bfloat16).reshape(experts, slot_cap, model_dim),
        "grp",
        split_axis=0,
        concat_axis=0,
        tiled=True,
    )
    weights = first_prob[:, None] * placed[:, 0, :] + second_prob[:, None] * placed[:, 1, :]
    contrib = jnp.dot(
        weights,
        returned.reshape(group_slots, model_dim).astype(jnp.float32),
        precision=HIGHEST_PREC,
    )
    return (hidden_float + contrib).astype(jnp.bfloat16)


def solution(mesh):
    torus = Mesh(mesh.devices.reshape(mesh.shape["grp"], 4, 8), ("grp", "dev_0", "dev_1"))
    in_specs = (
        P("grp", DEV),
        P("grp", DEV),
        P("grp", DEV),
        P(DEV),
        P("grp", None),
        P("grp", None),
        P(DEV),
        P(DEV),
        P(None, DEV),
        P(GRP_DEV, None),
        P(),
        P(),
        P(GRP_DEV, None),
        P("grp", None, DEV),
        P("grp", None, DEV),
        P("grp", DEV, None),
    )
    out_specs = P(GRP_DEV, None)
    return jax.shard_map(
        shards, mesh=torus, in_specs=in_specs, out_specs=out_specs, check_vma=False
    )
```

profile of v0, /device:TPU:1, one launch (start us, length us, event | category | flops | bytes accessed | tf_op | source)
XLA Modules:
  0.0 574.6 jit_solution(1486846018110611630)
XLA Ops:
  6.6 0.9 negate_bitcast_fusion
  7.5 0.6 reduce-window.6
  8.1 0.2 slice_reduce_fusion
  8.3 0.2 reduce-window.9
  8.5 0.2 slice_reduce_fusion.1
  8.8 0.8 fusion.58
  9.5 0.9 copy.61
  10.5 1.0 convolution_convert_fusion.2
  11.6 0.1 pad_maximum_fusion
  11.7 26.0 %all_gather.12 = bf16[16,2,8193]{2,1,0:T(2,128)(2,1)S(1)} all-gather(bf16[1,2,8193]{2,1,0:T(2,128)(2,1)S(1)} %pad_maximum_fusion), channel_id=1, replica_groups=mesh['grp'=16,'dev_0'=4,'dev_1'=8] {'grp'}, dimensions={0}, use_global_device_ids=true | all-gather | bytes 557124 | tf_op jit(solution)/shard_map/all_gather | solution.py:16
  37.6 0.7 slice.40
  38.4 0.1 copy.76
  38.5 0.1 copy.64
  38.6 0.1 select_reduce_fusion.1
  38.8 0.1 copy.73
  38.9 0.4 reshape.234
  39.3 1.1 fusion.59
  40.3 0.6 fusion.18
  40.9 0.2 fusion.4
  41.2 0.6 fusion.3
  41.8 0.1 copy.66
  41.9 0.1 multiply_reduce_fusion
  42.0 61.3 %psum.7 = f32[256]{0:T(256)S(1)} all-reduce(f32[256]{0:T(256)S(1)} %multiply_reduce_fusion), channel_id=1, replica_groups=mesh['grp'=16,'dev_0'=4,'dev_1'=8] {'dev_0','dev_1'}, use_global_device_ids=true, to_apply=%region_5.6 | all-reduce | flops 256 | bytes 2048 | tf_op jit(solution)/shard_map/psum | solution.py:144
  103.4 0.7 multiply_convert_fusion
  104.4 0.2 select_reduce_fusion
  104.7 0.1 copy.72
  104.7 81.8 %all-gather.6.cloned.1.call-done = bf16[8192,128]{1,0:T(8,128)(2,1)} async-done(((bf16[256,128]{1,0:T(8,128)(2,1)}), bf16[8192,128]{1,0:T(8,128)(2,1)}) %all-gather.6.cloned.1.call-update) | async-done | bytes 2097168 | tf_op jit(solution)/shard_map/all_gather | solution.py:148
  186.6 2.3 fusion.5
  188.9 0.1 copy.68
  189.1 0.7 reshape.251
  189.8 4.9 all-to-all-start
  194.9 8.6 %all-to-all-done = bf16[32,2,256]{2,1,0:T(2,128)(2,1)S(1)} async-done(((bf16[32,2,256]{2,1,0:T(2,128)(2,1)}), bf16[32,2,256]{2,1,0:T(2,128)(2,1)S(1)}, u32[]{:S(2)}, u32[]{:S(2)}) %all-to-all-start) | async-done | bytes 32800 | tf_op jit(solution)/shard_map/all_to_all | solution.py:155
  203.5 0.1 reshape.252
  203.7 0.1 reshape.242
  203.8 0.1 fusion.37
  203.9 0.2 convolution_convert_fusion.1
  204.2 0.1 reshape.237
  204.3 22.8 %all_to_all.23 = bf16[16,2,2048]{2,1,0:T(2,128)(2,1)} all-to-all(bf16[16,2,2048]{2,1,0:T(2,128)(2,1)S(1)} %reshape.237), channel_id=1, replica_groups=mesh['grp'=16,'dev_0'=4,'dev_1'=8] {'grp'}, dimensions={0} | all-to-all | bytes 262144 | tf_op jit(solution)/shard_map/all_to_all | solution.py:171
  227.1 73.9 %all-gather.4.cloned.1.call-done = bf16[512,2,2048]{2,1,0:T(2,128)(2,1)} async-done(((bf16[16,2,2048]{2,1,0:T(2,128)(2,1)}), bf16[512,2,2048]{2,1,0:T(2,128)(2,1)}) %all-gather.4.cloned.1.call-update) | async-done | bytes 4194320 | tf_op jit(solution)/shard_map/all_gather | solution.py:172
  301.0 7.2 %reshape.238 = bf16[1024,2048]{1,0:T(8,128)(2,1)} reshape(bf16[512,2,2048]{2,1,0:T(2,128)(2,1)} %all-gather.4.cloned.1.call-done) | data formatting | bytes 8388608 | tf_op jit(solution)/shard_map/reshape | solution.py:172
  308.2 4.5 fusion.9
  312.8 9.1 %convolution_convert_fusion = bf16[1024,2048]{1,0:T(8,128)(2,1)} fusion(bf16[1024,2048]{1,0:T(8,128)(2,1)} %reshape.238, bf16[1,256,2048]{2,1,0:T(8,128)(2,1)S(1)} %copy-done, bf16[1,2048,256]{2,1,0:T(8,128)(2,1)} %param.30, f32[1024,256]{1,0:T(8,128)} %fusion.9), kind=kOutput, calls=%fused_computation | convolution fusion | flops 2151153664 | bytes 11534336 | tf_op jit(solution)/shard_map/dot_general | solution.py:176
  322.0 222.0 %reduce-scatter.2.cloned.1.call-done = bf16[32,2048]{1,0:T(8,128)(2,1)} async-done(((bf16[1024,2048]{1,0:T(8,128)(2,1)}), bf16[32,2048]{1,0:T(8,128)(2,1)}) %reduce-scatter.2.cloned.1.call-update) | async-done | bytes 131088 | tf_op jit(solution)/shard_map/reduce_scatter | solution.py:48
  544.0 1.7 reshape.239
  545.6 12.4 %all-to-all-start.2 = ((bf16[16,2,2048]{2,1,0:T(2,128)(2,1)}), bf16[16,2,2048]{2,1,0:T(2,128)(2,1)S(1)}, u32[]{:S(2)}, u32[]{:S(2)}) async-start(bf16[16,2,2048]{2,1,0:T(2,128)(2,1)} %reshape.239), calls=%async_computation.3 | async-start | bytes 262144 | tf_op jit(solution)/shard_map/all_to_all | solution.py:177
  558.0 0.3 select_reduce_fusion.2
  558.4 8.8 %all-to-all-done.2 = bf16[16,2,2048]{2,1,0:T(2,128)(2,1)S(1)} async-done(((bf16[16,2,2048]{2,1,0:T(2,128)(2,1)}), bf16[16,2,2048]{2,1,0:T(2,128)(2,1)S(1)}, u32[]{:S(2)}, u32[]{:S(2)}) %all-to-all-start.2) | async-done | bytes 131104 | tf_op jit(solution)/shard_map/all_to_all | solution.py:177
  567.2 0.9 fusion
  (56 shorter events, 1.2 us)
Async XLA Ops:
  6.5 306.2 %copy-start = (bf16[1,256,2048]{2,1,0:T(8,128)(2,1)S(1)}, bf16[1,256,2048]{2,1,0:T(8,128)(2,1)}, u32[]{:S(2)}) copy-start(bf16[1,256,2048]{2,1,0:T(8,128)(2,1)} %param.31) | copy-start | bytes 3145732
  6.5 34.6 %copy-start.6 = (f32[256,2]{0,1:T(2,128)S(1)}, f32[256,2]{0,1:T(2,128)}, u32[]{:S(2)}) copy-start(f32[256,2]{0,1:T(2,128)} %param.18) | copy-start | bytes 6148
  6.5 34.4 %copy-start.3 = (bf16[256,128]{1,0:T(8,128)(2,1)S(1)}, bf16[256,128]{1,0:T(8,128)(2,1)}, u32[]{:S(2)}) copy-start(bf16[256,128]{1,0:T(8,128)(2,1)} %param.21) | copy-start | bytes 196612
  6.5 34.6 %copy-start.11 = (f32[2]{0:T(128)S(1)}, f32[2]{0:T(128)}, u32[]{:S(2)}) copy-start(f32[2]{0:T(128)} %param.22) | copy-start | bytes 28
  6.5 35.3 %copy-start.2 = (bf16[256,128]{1,0:T(8,128)(2,1)S(1)}, bf16[256,128]{1,0:T(8,128)(2,1)}, u32[]{:S(2)}) copy-start(bf16[256,128]{1,0:T(8,128)(2,1)} %param.17) | copy-start | bytes 196612
  6.5 96.8 %copy-start.8 = (f32[128]{0:T(128)S(1)}, f32[128]{0:T(128)}, u32[]{:S(2)}) copy-start(f32[128]{0:T(128)} %param.23) | copy-start | bytes 1540
  6.6 97.5 %copy-start.7 = (s32[8,2]{0,1:T(2,128)S(1)}, s32[8,2]{0,1:T(2,128)}, u32[]{:S(2)}) copy-start(s32[8,2]{0,1:T(2,128)} %param.28) | copy-start | bytes 196
  6.6 180.0 %copy-start.1 = (bf16[4096,64]{0,1:T(8,128)(2,1)S(1)}, bf16[4096,64]{0,1:T(8,128)(2,1)}, u32[]{:S(2)}) copy-start(bf16[4096,64]{0,1:T(8,128)(2,1)} %param.24) | copy-start | bytes 1572868
  6.6 180.0 %all-gather.6.cloned.1.call-start = ((), (), s32[]{:S(2)}) async-start(), calls=%async_computation.6 | async-start | bytes 2162688 | tf_op jit(solution)/shard_map/all_gather | solution.py:148
  38.3 165.4 %copy-start.4 = (bf16[8,2048]{1,0:T(8,128)(2,1)S(1)}, bf16[8,2048]{1,0:T(8,128)(2,1)}, u32[]{:S(2)}) copy-start(bf16[8,2048]{1,0:T(8,128)(2,1)} %param.25) | copy-start | bytes 98308
  38.7 165.2 %copy-start.5 = (f32[2048]{0:T(1024)S(1)}, f32[2048]{0:T(1024)}, u32[]{:S(2)}) copy-start(f32[2048]{0:T(1024)} %param.26) | copy-start | bytes 24580
  189.8 13.7 %all-to-all-start = ((bf16[32,2,256]{2,1,0:T(2,128)(2,1)}), bf16[32,2,256]{2,1,0:T(2,128)(2,1)S(1)}, u32[]{:S(2)}, u32[]{:S(2)}) async-start(bf16[32,2,256]{2,1,0:T(2,128)(2,1)} %reshape.251), calls=%async_computation | async-start | bytes 65536 | tf_op jit(solution)/shard_map/all_to_all | solution.py:155
  194.7 106.3 %all-gather.4.cloned.1.call-start = ((), (), s32[]{:S(2)}) async-start(), calls=%async_computation.4 | async-start | bytes 4325376 | tf_op jit(solution)/shard_map/all_gather | solution.py:172
  227.1 81.2 %copy-start.9 = (bf16[1,2048,256]{2,1,0:T(8,128)(2,1)S(1)}, bf16[1,2048,256]{2,1,0:T(8,128)(2,1)}, u32[]{:S(2)}) copy-start(bf16[1,2048,256]{2,1,0:T(8,128)(2,1)} %param.29) | copy-start | bytes 3145732
  227.1 316.9 %reduce-scatter.2.cloned.1.call-start = ((), (), s32[]{:S(2)}) async-start(), calls=%async_computation.5 | async-start | bytes 4325376 | tf_op jit(solution)/shard_map/reduce_scatter | solution.py:48
  321.9 236.1 %copy-start.10 = (f32[2048,16]{0,1:T(8,128)S(1)}, f32[2048,16]{0,1:T(8,128)}, u32[]{:S(2)}) copy-start(f32[2048,16]{0,1:T(8,128)} %param.27) | copy-start | bytes 393220
  545.6 21.6 %all-to-all-start.2 = ((bf16[16,2,2048]{2,1,0:T(2,128)(2,1)}), bf16[16,2,2048]{2,1,0:T(2,128)(2,1)S(1)}, u32[]{:S(2)}, u32[]{:S(2)}) async-start(bf16[16,2,2048]{2,1,0:T(2,128)(2,1)} %reshape.239), calls=%async_computation.3 | async-start | bytes 262144 | tf_op jit(solution)/shard_map/all_to_all | solution.py:177
Sparse Core Ops, SparseCore 0:
  104.2 82.3 all-gather.5
  227.2 73.7 all-gather.3
  322.0 221.9 reduce-scatter.1
where the time goes:
time: 575 us
  waiting for transfers between devices  395 us (69%)
  blocking collectives  110 us (19%)
  matrix products  20.9 us (4%)
  starting transfers between devices  17.4 us (3%)
  between operations  13.4 us (2%)
  local copies, waits for them, and re-layouts  13.3 us (2%)
    reduce_scatter x1, waiting for transfers between devices, sum_by_axis(): total = lax.psum_scatter(total, axes, scatter_dimension=0, tiled=True)  222 us
    all_gather x1, waiting for transfers between devices, shards(): gathered = lax.all_gather(mixed_rows, DEV, axis=0)  81.8 us
    all_gather x1, waiting for transfers between devices, shards(): lax.all_gather(arrived, DEV, axis=0, tiled=True).reshape(-1, model_dim)  73.9 us
    psum x1, blocking collectives, shards(): squares = lax.psum(jnp.sum(gated_out * gated_out, axis=1), DEV)  61.3 us
    all_gather x1, blocking collectives, side_by_side(): lax.all_gather(both, axis, axis=dim, tiled=True)  26 us
    all_to_all x1, blocking collectives, shards(): lax.all_to_all(outgoing, 'grp', split_axis=0, concat_axis=0, tiled=True)  22.8 us
    all_to_all x1, starting transfers between devices, shards(): lax.all_to_all(summed.astype(jnp.bfloat16).reshape(experts, slot_cap, mod...  12.4 us
  transfers between devices with their start and end apart: 5, of which 5 were waited for; matrix products, arithmetic and copies ran while one was open for 0% of the time, Pallas kernels for 0%

commit v1 on v0

--- a/solution.py
+++ b/solution.py
@@ -141,7 +141,7 @@
     gated_out = ssm_out.reshape(tok_rows, head_count * head_width) * jax.nn.silu(
         gate_input.astype(jnp.float32)
     )
-    squares = lax.psum(jnp.sum(gated_out * gated_out, axis=1), DEV)
+    squares = lax.psum(lax.psum(jnp.sum(gated_out * gated_out, axis=1), "dev_1"), "dev_0")
     mixed_rows = (
         gated_out * lax.rsqrt(squares[:, None] / inner_dim + EPSILON) * norm_gain[None, :]
     ).astype(jnp.bfloat16)

time: 575 us -> 531 us (0.923)
  blocking collectives: 110 us -> 71.1 us
    psum x1 -> x2, blocking collectives: 61.3 us -> 22.4 us  [the longest x1 13.9 us: shards(): lax.psum(jnp.sum(gated_out * gated_out, axis=1), 'dev_1')]
where the time goes in v1:
time: 531 us; the launch traced here: 530 us
  waiting for transfers between devices  390 us (73%)
  blocking collectives  71.1 us (13%)
  matrix products  20.9 us (4%)
  starting transfers between devices  17.5 us (3%)
  between operations  13.4 us (3%)
  local copies, waits for them, and re-layouts  13.3 us (3%)
    reduce_scatter x1, waiting for transfers between devices, sum_by_axis(): total = lax.psum_scatter(total, axes, scatter_dimension=0, tiled=True)  222 us
    all_gather x1, waiting for transfers between devices, shards(): gathered = lax.all_gather(mixed_rows, DEV, axis=0)  76.4 us
    all_gather x1, waiting for transfers between devices, shards(): lax.all_gather(arrived, DEV, axis=0, tiled=True).reshape(-1, model_dim)  73.9 us
    all_gather x1, blocking collectives, side_by_side(): lax.all_gather(both, axis, axis=dim, tiled=True)  26 us
    all_to_all x1, blocking collectives, shards(): lax.all_to_all(outgoing, 'grp', split_axis=0, concat_axis=0, tiled=True)  22.8 us
    psum x1, blocking collectives, shards(): lax.psum(jnp.sum(gated_out * gated_out, axis=1), 'dev_1')  13.9 us
    all_to_all x1, starting transfers between devices, shards(): lax.all_to_all(summed.astype(jnp.bfloat16).reshape(experts, slot_cap, mod...  12.4 us
  transfers between devices with their start and end apart: 5, of which 5 were waited for; matrix products, arithmetic and copies ran while one was open for 0% of the time, Pallas kernels for 0%

profile of v1, /device:TPU:1, one launch (start us, length us, event | category | flops | bytes accessed | tf_op | source)
XLA Modules:
  0.0 530.2 jit_solution(914711496053147012)
XLA Ops:
  6.6 0.9 negate_bitcast_fusion
  7.5 0.6 reduce-window.6
  8.1 0.2 slice_reduce_fusion
  8.3 0.2 reduce-window.9
  8.5 0.2 slice_reduce_fusion.1
  8.8 0.8 fusion.58
  9.5 0.9 copy.61
  10.5 1.0 convolution_convert_fusion.2
  11.6 0.1 pad_maximum_fusion
  11.7 26.0 %all_gather.12 = bf16[16,2,8193]{2,1,0:T(2,128)(2,1)S(1)} all-gather(bf16[1,2,8193]{2,1,0:T(2,128)(2,1)S(1)} %pad_maximum_fusion), channel_id=1, replica_groups=mesh['grp'=16,'dev_0'=4,'dev_1'=8] {'grp'}, dimensions={0}, use_global_device_ids=true | all-gather | bytes 557124 | tf_op jit(solution)/shard_map/all_gather | solution.py:16
  37.6 0.7 slice.40
  38.4 0.1 copy.76
  38.5 0.1 copy.64
  38.6 0.1 select_reduce_fusion.1
  38.9 0.4 reshape.234
  39.3 1.1 fusion.59
  40.3 0.6 fusion.18
  40.9 0.2 fusion.4
  41.2 0.6 fusion.3
  41.8 0.1 copy.66
  41.9 0.1 multiply_reduce_fusion
  42.0 13.9 %psum.14 = f32[256]{0:T(256)S(1)} all-reduce(f32[256]{0:T(256)S(1)} %multiply_reduce_fusion), channel_id=1, replica_groups=mesh['grp'=16,'dev_0'=4,'dev_1'=8] {'dev_1'}, use_global_device_ids=true, to_apply=%region_5.6 | all-reduce | flops 256 | bytes 2048 | tf_op jit(solution)/shard_map/psum | solution.py:144
  55.9 8.5 %psum.15 = f32[256]{0:T(256)S(1)} all-reduce(f32[256]{0:T(256)S(1)} %psum.14), channel_id=1, replica_groups=mesh['grp'=16,'dev_0'=4,'dev_1'=8] {'dev_0'}, use_global_device_ids=true, to_apply=%region_6.7 | all-reduce | flops 256 | bytes 2048 | tf_op jit(solution)/shard_map/psum | solution.py:144
  64.4 0.7 multiply_convert_fusion
  65.4 0.2 select_reduce_fusion
  65.7 0.1 copy.72
  65.8 76.4 %all-gather.6.cloned.1.call-done = bf16[8192,128]{1,0:T(8,128)(2,1)} async-done(((bf16[256,128]{1,0:T(8,128)(2,1)}), bf16[8192,128]{1,0:T(8,128)(2,1)}) %all-gather.6.cloned.1.call-update) | async-done | bytes 2097168 | tf_op jit(solution)/shard_map/all_gather | solution.py:148
  142.2 2.3 fusion.5
  144.5 0.1 copy.68
  144.6 0.7 reshape.251
  145.4 4.9 all-to-all-start
  150.5 8.6 %all-to-all-done = bf16[32,2,256]{2,1,0:T(2,128)(2,1)S(1)} async-done(((bf16[32,2,256]{2,1,0:T(2,128)(2,1)}), bf16[32,2,256]{2,1,0:T(2,128)(2,1)S(1)}, u32[]{:S(2)}, u32[]{:S(2)}) %all-to-all-start) | async-done | bytes 32800 | tf_op jit(solution)/shard_map/all_to_all | solution.py:155
  159.1 0.1 reshape.252
  159.3 0.1 reshape.242
  159.4 0.1 fusion.37
  159.5 0.2 convolution_convert_fusion.1
  159.8 0.1 reshape.237
  159.9 22.8 %all_to_all.23 = bf16[16,2,2048]{2,1,0:T(2,128)(2,1)} all-to-all(bf16[16,2,2048]{2,1,0:T(2,128)(2,1)S(1)} %reshape.237), channel_id=1, replica_groups=mesh['grp'=16,'dev_0'=4,'dev_1'=8] {'grp'}, dimensions={0} | all-to-all | bytes 262144 | tf_op jit(solution)/shard_map/all_to_all | solution.py:171
  182.7 73.9 %all-gather.4.cloned.1.call-done = bf16[512,2,2048]{2,1,0:T(2,128)(2,1)} async-done(((bf16[16,2,2048]{2,1,0:T(2,128)(2,1)}), bf16[512,2,2048]{2,1,0:T(2,128)(2,1)}) %all-gather.4.cloned.1.call-update) | async-done | bytes 4194320 | tf_op jit(solution)/shard_map/all_gather | solution.py:172
  256.6 7.2 %reshape.238 = bf16[1024,2048]{1,0:T(8,128)(2,1)} reshape(bf16[512,2,2048]{2,1,0:T(2,128)(2,1)} %all-gather.4.cloned.1.call-done) | data formatting | bytes 8388608 | tf_op jit(solution)/shard_map/reshape | solution.py:172
  263.8 4.5 fusion.9
  268.3 9.1 %convolution_convert_fusion = bf16[1024,2048]{1,0:T(8,128)(2,1)} fusion(bf16[1024,2048]{1,0:T(8,128)(2,1)} %reshape.238, bf16[1,256,2048]{2,1,0:T(8,128)(2,1)S(1)} %copy-done, bf16[1,2048,256]{2,1,0:T(8,128)(2,1)} %param.30, f32[1024,256]{1,0:T(8,128)} %fusion.9), kind=kOutput, calls=%fused_computation | convolution fusion | flops 2151153664 | bytes 11534336 | tf_op jit(solution)/shard_map/dot_general | solution.py:176
  277.6 222.0 %reduce-scatter.2.cloned.1.call-done = bf16[32,2048]{1,0:T(8,128)(2,1)} async-done(((bf16[1024,2048]{1,0:T(8,128)(2,1)}), bf16[32,2048]{1,0:T(8,128)(2,1)}) %reduce-scatter.2.cloned.1.call-update) | async-done | bytes 131088 | tf_op jit(solution)/shard_map/reduce_scatter | solution.py:48
  499.5 1.7 reshape.239
  501.2 12.4 %all-to-all-start.2 = ((bf16[16,2,2048]{2,1,0:T(2,128)(2,1)}), bf16[16,2,2048]{2,1,0:T(2,128)(2,1)S(1)}, u32[]{:S(2)}, u32[]{:S(2)}) async-start(bf16[16,2,2048]{2,1,0:T(2,128)(2,1)} %reshape.239), calls=%async_computation.3 | async-start | bytes 262144 | tf_op jit(solution)/shard_map/all_to_all | solution.py:177
  513.6 0.3 select_reduce_fusion.2
  514.0 8.8 %all-to-all-done.2 = bf16[16,2,2048]{2,1,0:T(2,128)(2,1)S(1)} async-done(((bf16[16,2,2048]{2,1,0:T(2,128)(2,1)}), bf16[16,2,2048]{2,1,0:T(2,128)(2,1)S(1)}, u32[]{:S(2)}, u32[]{:S(2)}) %all-to-all-start.2) | async-done | bytes 131104 | tf_op jit(solution)/shard_map/all_to_all | solution.py:177
  522.8 0.9 fusion
  (57 shorter events, 1.3 us)
Async XLA Ops:
  6.5 261.8 %copy-start = (bf16[1,256,2048]{2,1,0:T(8,128)(2,1)S(1)}, bf16[1,256,2048]{2,1,0:T(8,128)(2,1)}, u32[]{:S(2)}) copy-start(bf16[1,256,2048]{2,1,0:T(8,128)(2,1)} %param.31) | copy-start | bytes 3145732
  6.5 34.6 %copy-start.6 = (f32[256,2]{0,1:T(2,128)S(1)}, f32[256,2]{0,1:T(2,128)}, u32[]{:S(2)}) copy-start(f32[256,2]{0,1:T(2,128)} %param.18) | copy-start | bytes 6148
  6.5 34.4 %copy-start.3 = (bf16[256,128]{1,0:T(8,128)(2,1)S(1)}, bf16[256,128]{1,0:T(8,128)(2,1)}, u32[]{:S(2)}) copy-start(bf16[256,128]{1,0:T(8,128)(2,1)} %param.21) | copy-start | bytes 196612
  6.5 34.6 %copy-start.11 = (f32[2]{0:T(128)S(1)}, f32[2]{0:T(128)}, u32[]{:S(2)}) copy-start(f32[2]{0:T(128)} %param.22) | copy-start | bytes 28
  6.5 35.3 %copy-start.2 = (bf16[256,128]{1,0:T(8,128)(2,1)S(1)}, bf16[256,128]{1,0:T(8,128)(2,1)}, u32[]{:S(2)}) copy-start(bf16[256,128]{1,0:T(8,128)(2,1)} %param.17) | copy-start | bytes 196612
  6.5 57.9 %copy-start.8 = (f32[128]{0:T(128)S(1)}, f32[128]{0:T(128)}, u32[]{:S(2)}) copy-start(f32[128]{0:T(128)} %param.23) | copy-start | bytes 1540
  6.6 58.6 %copy-start.7 = (s32[8,2]{0,1:T(2,128)S(1)}, s32[8,2]{0,1:T(2,128)}, u32[]{:S(2)}) copy-start(s32[8,2]{0,1:T(2,128)} %param.28) | copy-start | bytes 196
  6.6 135.6 %copy-start.1 = (bf16[4096,64]{0,1:T(8,128)(2,1)S(1)}, bf16[4096,64]{0,1:T(8,128)(2,1)}, u32[]{:S(2)}) copy-start(bf16[4096,64]{0,1:T(8,128)(2,1)} %param.24) | copy-start | bytes 1572868
  6.6 135.6 %all-gather.6.cloned.1.call-start = ((), (), s32[]{:S(2)}) async-start(), calls=%async_computation.6 | async-start | bytes 2162688 | tf_op jit(solution)/shard_map/all_gather | solution.py:148
  38.3 121.0 %copy-start.4 = (bf16[8,2048]{1,0:T(8,128)(2,1)S(1)}, bf16[8,2048]{1,0:T(8,128)(2,1)}, u32[]{:S(2)}) copy-start(bf16[8,2048]{1,0:T(8,128)(2,1)} %param.25) | copy-start | bytes 98308
  38.7 120.8 %copy-start.5 = (f32[2048]{0:T(1024)S(1)}, f32[2048]{0:T(1024)}, u32[]{:S(2)}) copy-start(f32[2048]{0:T(1024)} %param.26) | copy-start | bytes 24580
  145.4 13.7 %all-to-all-start = ((bf16[32,2,256]{2,1,0:T(2,128)(2,1)}), bf16[32,2,256]{2,1,0:T(2,128)(2,1)S(1)}, u32[]{:S(2)}, u32[]{:S(2)}) async-start(bf16[32,2,256]{2,1,0:T(2,128)(2,1)} %reshape.251), calls=%async_computation | async-start | bytes 65536 | tf_op jit(solution)/shard_map/all_to_all | solution.py:155
  150.3 106.3 %all-gather.4.cloned.1.call-start = ((), (), s32[]{:S(2)}) async-start(), calls=%async_computation.4 | async-start | bytes 4325376 | tf_op jit(solution)/shard_map/all_gather | solution.py:172
  182.7 81.2 %copy-start.9 = (bf16[1,2048,256]{2,1,0:T(8,128)(2,1)S(1)}, bf16[1,2048,256]{2,1,0:T(8,128)(2,1)}, u32[]{:S(2)}) copy-start(bf16[1,2048,256]{2,1,0:T(8,128)(2,1)} %param.29) | copy-start | bytes 3145732
  182.7 316.9 %reduce-scatter.2.cloned.1.call-start = ((), (), s32[]{:S(2)}) async-start(), calls=%async_computation.5 | async-start | bytes 4325376 | tf_op jit(solution)/shard_map/reduce_scatter | solution.py:48
  277.4 236.1 %copy-start.10 = (f32[2048,16]{0,1:T(8,128)S(1)}, f32[2048,16]{0,1:T(8,128)}, u32[]{:S(2)}) copy-start(f32[2048,16]{0,1:T(8,128)} %param.27) | copy-start | bytes 393220
  501.2 21.6 %all-to-all-start.2 = ((bf16[16,2,2048]{2,1,0:T(2,128)(2,1)}), bf16[16,2,2048]{2,1,0:T(2,128)(2,1)S(1)}, u32[]{:S(2)}, u32[]{:S(2)}) async-start(bf16[16,2,2048]{2,1,0:T(2,128)(2,1)} %reshape.239), calls=%async_computation.3 | async-start | bytes 262144 | tf_op jit(solution)/shard_map/all_to_all | solution.py:177
Sparse Core Ops, SparseCore 0:
  65.3 76.8 all-gather.5
  182.8 73.7 all-gather.3
  277.6 221.9 reduce-scatter.1
